TPU v7x, 32 devices: a whole 2x2x4 slice. The times are simulated.
32 devices in a mesh: pw: 8 (over z, y), band: 4 (over x, core).
Axes of the slice: x: 2, y: 2, z: 4, core: 2. Of those that a mesh axis runs over, the one named last changes fastest.
Arguments:
- psi_block: float32 [2, 8, 256, 128], P(None, 'band', 'pw'), may hold values from -6 to 6
- psi_all: bfloat16 [2, 1024, 256, 128], P(None, 'band', 'pw'), may hold values from -0.0234375 to 0.0234375
- potential: float32 [128, 128, 128], P('pw'), may hold values from -8 to 8
- stick_col: int32 [256], replicated, may hold values from 0 to 16383, as said below
Outputs:
- intersection: float32 [2, 8, 1024], P(None, 'pw', 'band')
- hpsi: float32 [2, 8, 256, 128], P(None, 'band', 'pw')
Inputs may be any that keep to these rules, and one draw needn't show every extreme that they name: `stick_col`: distinct columns of the 128 x 128 plane; column 0 and column 16383 are always among them.
All inputs are finite; a program needn't handle non-finite values.
Results may differ from a plain program's by a relative error of at most 0.0029.
Values may be sent and summed in bfloat16 or wider, within the bound.
No kernel may reach another device: no remote copies, remote signals or barrier semaphores. Data moves between devices by JAX's collectives and lax.ppermute only.
A program may use at most 64 MiB of HBM per device.

v0:
```python
import math
import jax
import jax.numpy as jnp
from jax import lax
from jax.sharding import PartitionSpec as P


def frequency(index, size):
    return jnp.where(index < size // 2, index, index - size)


def kinetic_table(columns, grid_size):
    col_x = frequency(columns // grid_size, grid_size).astype(jnp.float32)
    col_y = frequency(columns % grid_size, grid_size).astype(jnp.float32)
    along = frequency(jnp.arange(grid_size, dtype=jnp.int32), grid_size).astype(jnp.float32)
    plane = col_x * col_x + col_y * col_y
    return 4.0 * (plane[:, None] + along[None, :] * along[None, :]) / float(grid_size * grid_size)


def dft_table(grid_size, sign):
    indices = jnp.arange(grid_size, dtype=jnp.int32)
    products = indices[:, None] * indices[None, :] % grid_size
    angles = 2.0 * math.pi / grid_size * products.astype(jnp.float32)
    cosine = jnp.cos(angles)
    sine = sign * jnp.sin(angles)
    return jnp.stack([jnp.stack([cosine, -sine]), jnp.stack([sine, cosine])])


def per_device(psi_block, psi_all, potential, stick_col):
    local_bands = psi_block.shape[1]
    sticks_dev = psi_block.shape[2]
    grid_size = psi_block.shape[3]
    highest = lax.Precision.HIGHEST
    rank = lax.axis_index("pw")
    pw_count = lax.axis_size("pw")
    band_count = lax.axis_size("band")
    my_columns = lax.dynamic_slice_in_dim(stick_col, rank * sticks_dev, sticks_dev)
    kinetic = kinetic_table(my_columns, grid_size)
    inverse = dft_table(grid_size, 1.0)
    forward = dft_table(grid_size, -1.0)
    cosine = inverse[0, 0]
    sine = inverse[1, 0]
    grid_iota = jnp.arange(grid_size, dtype=jnp.int32)
    col_x = stick_col // grid_size
    col_y = stick_col % grid_size
    phase_angles = (
        2.0
        * math.pi
        / grid_size
        * (grid_iota[:, None] * col_y[None, :] % grid_size).astype(jnp.float32)
    )
    phase_cos = jnp.cos(phase_angles)
    phase_sin = jnp.sin(phase_angles)
    place_rows = (col_x[:, None] == grid_iota[None, :]).astype(jnp.float32)
    pick_rows = (grid_iota[:, None] == col_x[None, :]).astype(jnp.float32)
    turned_pot = (jnp.transpose(potential, (0, 2, 1)) / float(grid_size**3))[None]

    def mult(left, right):
        return jnp.dot(left, right, precision=highest, preferred_element_type=jnp.float32)

    all_re = psi_all[0].reshape(psi_all.shape[1], -1)
    all_im = psi_all[1].reshape(psi_all.shape[1], -1)
    dims = (((1,), (1,)), ((), ()))
    group_count = local_bands // 2
    z_lines = jnp.einsum("dcvu,cbsu->bvds", inverse, psi_block, precision=highest)
    planes_in = lax.all_to_all(z_lines, "pw", split_axis=1, concat_axis=3, tiled=True)
    val_re = planes_in[:, :, 0, None, :]
    val_im = planes_in[:, :, 1, None, :]
    spread_re = val_re * phase_cos - val_im * phase_sin
    spread_im = val_re * phase_sin + val_im * phase_cos
    rows_re = mult(spread_re, place_rows)
    rows_im = mult(spread_im, place_rows)
    wave_re = (mult(rows_re, cosine) - mult(rows_im, sine)) * turned_pot
    wave_im = (mult(rows_re, sine) + mult(rows_im, cosine)) * turned_pot
    back_re = mult(wave_re, cosine) + mult(wave_im, sine)
    back_im = mult(wave_im, cosine) - mult(wave_re, sine)
    sel_re = mult(back_re, pick_rows)
    sel_im = mult(back_im, pick_rows)
    picked_re = jnp.sum(sel_re * phase_cos + sel_im * phase_sin, axis=2)
    picked_im = jnp.sum(sel_im * phase_cos - sel_re * phase_sin, axis=2)
    picked = jnp.stack([picked_re, picked_im], axis=2)
    sticks_back = lax.all_to_all(picked, "pw", split_axis=3, concat_axis=1, tiled=True)
    vpsi = jnp.einsum("dcvu,bucs->dbsv", forward, sticks_back, precision=highest)
    applied = kinetic[None, None] * psi_block + vpsi
    lowered = applied.astype(jnp.bfloat16)
    gathered = lax.all_gather(lowered, "band", axis=1, tiled=True)
    h_re = gathered[0].reshape(gathered.shape[1], -1)
    h_im = gathered[1].reshape(gathered.shape[1], -1)
    real_part = lax.dot_general(
        h_re, all_re, dims, preferred_element_type=jnp.float32
    ) + lax.dot_general(h_im, all_im, dims, preferred_element_type=jnp.float32)
    imag_part = lax.dot_general(
        h_re, all_im, dims, preferred_element_type=jnp.float32
    ) - lax.dot_general(h_im, all_re, dims, preferred_element_type=jnp.float32)
    partials = [jnp.stack([real_part, imag_part])]
    stacked = jnp.stack(partials, axis=1)
    stacked = stacked.reshape(2, group_count, band_count, 2, stacked.shape[-1])
    partial_value = jnp.transpose(stacked, (0, 2, 1, 3, 4)).reshape(
        2, band_count * local_bands, stacked.shape[-1]
    )
    summed = lax.psum(partial_value, "pw")
    cols_dev = partial_value.shape[1] // pw_count
    intersection = lax.dynamic_slice_in_dim(summed, rank * cols_dev, cols_dev, 1)
    return (intersection, applied)


def solution(mesh):
    return jax.shard_map(
        per_device,
        mesh=mesh,
        in_specs=(
            P(None, "band", "pw", None),
            P(None, "band", "pw", None),
            P("pw", None, None),
            P(),
        ),
        out_specs=(P(None, "pw", "band"), P(None, "band", "pw", None)),
        check_vma=False,
    )
```

profile of v0, /device:TPU:0, one launch (start us, length us, event | category | flops | bytes accessed | tf_op | source)
XLA Modules:
  0.0 115.9 jit_solution(15763958665738720233)
XLA Ops:
  0.6 0.0 copy-start.6
  0.6 0.0 copy-start.2
  0.6 0.3 fusion.76
  0.9 0.3 fusion.74
  1.2 0.3 broadcast_multiply_fusion
  1.5 0.7 fusion.40
  2.2 1.2 %convolution_bitcast_fusion = f32[2,128,2,32]{1,3,0,2:T(8,128)S(1)} fusion(f32[1,2,128,128]{3,2,1,0:T(8,128)S(1)} %get-tuple-element.20, f32[1,2,128,128]{3,2,1,0:T(8,128)S(1)} %get-tuple-element.21, f32[2,2,32,128]{3,2,1,0:T(8,128)} %param.4), kind=kOutput, calls=%fused_computation.30 | convolution fusion | flops 50397184 | bytes 393216 | tf_op jit(solution)/shard_map/dcvu,cbsu->bvds/dot_general | solution.py:65
  3.4 0.2 copy.63
  3.6 0.9 reshape.230
  4.5 7.3 %all-to-all-start = ((f32[8,1,2048]{2,1,0:T(1,128)}), f32[8,1,2048]{2,1,0:T(1,128)}, u32[]{:S(2)}, u32[]{:S(2)}) async-start(f32[8,1,2048]{2,1,0:T(1,128)} %reshape.230), calls=%async_computation | async-start | bytes 131072 | tf_op jit(solution)/shard_map/all_to_all | solution.py:66
  11.8 0.0 copy-done.6
  11.8 1.2 %fusion.62 = (f32[128,256]{1,0:T(8,128)S(1)}, f32[128,256]{1,0:T(8,128)}) fusion(s32[256]{0:T(256)S(1)} %get-tuple-element.25), kind=kLoop, calls=%fused_computation.86 | loop fusion | flops 458752 | bytes 263168 | tf_op jit(solution)/shard_map/cos | solution.py:52
  13.0 0.0 copy-done.2
  13.0 1.1 multiply_bitcast_fusion
  14.1 4.3 %fusion.86 = (bf16[1,256,32,128]{3,2,1,0:T(8,128)(2,1)S(1)}, bf16[1,256,32,128]{3,2,1,0:T(8,128)(2,1)}) fusion(bf16[2,256,32,128]{3,2,1,0:T(8,128)(2,1)} %param.5), kind=kLoop, calls=%fused_computation.131 | loop fusion | bytes 8388608 | tf_op jit(solution)/shard_map/slice | solution.py:61
  18.4 1.6 %copy.66 = f32[16,128,128]{2,1,0:T(8,128)S(1)} copy(f32[16,128,128]{1,2,0:T(8,128)} %multiply_bitcast_fusion) | data formatting | bytes 2097152 | tf_op jit(solution)/shard_map/div | solution.py:56
  20.0 0.1 fusion.79
  20.1 0.0 all-to-all-done
  20.1 0.5 broadcast.384
  20.6 2.3 %reduce = f32[8,2048]{1,0:T(8,128)} reduce(f32[8,1,2048]{2,1,0:T(1,128)} %all-to-all-done, f32[]{:T(128)} %broadcast.384), dimensions={1}, to_apply=%all_to_all.26.reduce_sub_computation | reduce | bytes 131076 | tf_op jit(solution)/shard_map/all_to_all | solution.py:66
  22.8 1.8 %reshape.231 = f32[128,2,2,32]{3,2,1,0:T(2,128)} reshape(f32[8,2048]{1,0:T(8,128)} %reduce) | data formatting | bytes 131072
  24.6 1.0 copy.64
  25.6 0.8 copy.65
  26.4 1.7 %all_to_all.29 = f32[2,16,2,256]{3,1,2,0:T(8,128)} reshape(f32[2,16,2,8,32]{4,3,1,2,0:T(8,128)} %copy.65) | data formatting | bytes 131072 | tf_op jit(solution)/shard_map/all_to_all | solution.py:66
  28.1 0.0 copy-start.1
  28.1 0.8 slice_bitcast_fusion.11
  28.9 3.3 %fusion = f32[2,16,128,128]{3,2,1,0:T(8,128)S(1)} fusion(f32[128,256]{1,0:T(8,128)} %get-tuple-element.27, f32[2,16,256]{2,1,0:T(8,128)S(1)} %get-tuple-element.23, f32[128,256]{1,0:T(8,128)S(1)} %get-tuple-element.26, f32[2,16,256]{2,1,0:T(8,128)S(1)} %get-tuple-element.22, s32[256]{0:T(256)S(1)} %get-tuple-element.24), kind=kOutput, calls=%fused_computation.2 | convolution fusion | flops 1613791232 | bytes 2425856 | tf_op jit(solution)/shard_map/dot_general | solution.py:59
  32.3 0.0 copy-done.1
  32.3 2.5 %fusion.4 = f32[2,16,128,128]{3,2,1,0:T(8,128)S(1)} fusion(f32[128,256]{1,0:T(8,128)S(1)} %copy-done.1, f32[2,16,256]{2,1,0:T(8,128)S(1)} %get-tuple-element.23, f32[128,256]{1,0:T(8,128)S(1)} %get-tuple-element.26, f32[2,16,256]{2,1,0:T(8,128)S(1)} %get-tuple-element.22, s32[256]{0:T(256)S(1)} %get-tuple-element.24), kind=kOutput, calls=%fused_computation.6 | convolution fusion | flops 1613791232 | bytes 2425856 | tf_op jit(solution)/shard_map/dot_general | solution.py:59
  34.7 1.9 %fusion.72 = f32[2,16,128,128]{3,2,1,0:T(8,128)S(1)} fusion(f32[2,16,128,128]{3,2,1,0:T(8,128)S(1)} %fusion.4, f32[1,2,128,128]{3,2,1,0:T(8,128)S(1)} %get-tuple-element.20), kind=kOutput, calls=%fused_computation.96 | convolution fusion | flops 805306368 | bytes 4259840 | tf_op jit(solution)/shard_map/dot_general | solution.py:59
  36.6 1.8 %fusion.69 = f32[2,16,128,128]{3,2,1,0:T(8,128)S(1)} fusion(f32[2,16,128,128]{3,2,1,0:T(8,128)S(1)} %fusion.4, f32[1,2,128,128]{3,2,1,0:T(8,128)S(1)} %get-tuple-element.21), kind=kOutput, calls=%fused_computation.93 | convolution fusion | flops 805306368 | bytes 4259840 | tf_op jit(solution)/shard_map/dot_general | solution.py:59
  38.4 2.0 %subtract_multiply_fusion = f32[2,16,128,128]{3,2,1,0:T(8,128)S(1)} fusion(f32[2,16,128,128]{3,2,1,0:T(8,128)S(1)} %fusion.69, f32[2,16,128,128]{3,2,1,0:T(8,128)S(1)} %fusion, f32[16,128,128]{2,1,0:T(8,128)S(1)} %copy.66, f32[1,2,128,128]{3,2,1,0:T(8,128)S(1)} %get-tuple-element.20), kind=kOutput, calls=%fused_computation.17 | convolution fusion | flops 806354944 | bytes 7405568 | tf_op jit(solution)/shard_map/dot_general | solution.py:59
  40.4 1.8 %fusion.70 = f32[2,16,128,128]{3,2,1,0:T(8,128)S(1)} fusion(f32[2,16,128,128]{3,2,1,0:T(8,128)S(1)} %subtract_multiply_fusion, f32[1,2,128,128]{3,2,1,0:T(8,128)S(1)} %get-tuple-element.20), kind=kOutput, calls=%fused_computation.94 | convolution fusion | flops 805306368 | bytes 4259840 | tf_op jit(solution)/shard_map/dot_general | solution.py:59
  42.2 1.8 %fusion.68 = f32[2,16,128,128]{3,2,1,0:T(8,128)S(1)} fusion(f32[2,16,128,128]{3,2,1,0:T(8,128)S(1)} %subtract_multiply_fusion, f32[1,2,128,128]{3,2,1,0:T(8,128)S(1)} %get-tuple-element.21), kind=kOutput, calls=%fused_computation.92 | convolution fusion | flops 805306368 | bytes 4259840 | tf_op jit(solution)/shard_map/dot_general | solution.py:59
  44.0 1.9 %add_multiply_fusion = f32[2,16,128,128]{3,2,1,0:T(8,128)S(1)} fusion(f32[2,16,128,128]{3,2,1,0:T(8,128)S(1)} %fusion.72, f32[2,16,128,128]{3,2,1,0:T(8,128)S(1)} %fusion, f32[16,128,128]{2,1,0:T(8,128)S(1)} %copy.66, f32[1,2,128,128]{3,2,1,0:T(8,128)S(1)} %get-tuple-element.21), kind=kOutput, calls=%fused_computation.16 | convolution fusion | flops 806354944 | bytes 7405568 | tf_op jit(solution)/shard_map/dot_general | solution.py:59
  46.0 1.8 %fusion.67 = f32[2,16,128,128]{3,2,1,0:T(8,128)S(1)} fusion(f32[2,16,128,128]{3,2,1,0:T(8,128)S(1)} %add_multiply_fusion, f32[1,2,128,128]{3,2,1,0:T(8,128)S(1)} %get-tuple-element.21), kind=kOutput, calls=%fused_computation.91 | convolution fusion | flops 805306368 | bytes 4259840 | tf_op jit(solution)/shard_map/dot_general | solution.py:59
  47.7 1.8 %fusion.71 = f32[2,16,128,128]{3,2,1,0:T(8,128)S(1)} fusion(f32[2,16,128,128]{3,2,1,0:T(8,128)S(1)} %add_multiply_fusion, f32[1,2,128,128]{3,2,1,0:T(8,128)S(1)} %get-tuple-element.20), kind=kOutput, calls=%fused_computation.95 | convolution fusion | flops 805306368 | bytes 4259840 | tf_op jit(solution)/shard_map/dot_general | solution.py:59
  49.6 1.8 %fusion.10 = f32[2,16,128,256]{3,2,1,0:T(8,128)S(1)} fusion(f32[2,16,128,128]{3,2,1,0:T(8,128)S(1)} %fusion.68, f32[2,16,128,128]{3,2,1,0:T(8,128)S(1)} %fusion.71, s32[256]{0:T(256)S(1)} %get-tuple-element.24), kind=kOutput, calls=%fused_computation.14 | convolution fusion | flops 1611169792 | bytes 8389632 | tf_op jit(solution)/shard_map/dot_general | solution.py:59
  51.4 2.8 %add_reduce_fusion = (f32[2,16,256]{2,1,0:T(8,128)S(1)}, f32[2,16,256]{2,1,0:T(8,128)S(1)}) fusion(f32[2,16,128,256]{3,2,1,0:T(8,128)S(1)} %fusion.10, f32[128,256]{1,0:T(8,128)S(1)} %copy-done.1, f32[128,256]{1,0:T(8,128)S(1)} %get-tuple-element.26, s32[256]{0:T(256)S(1)} %get-tuple-element.24, f32[2,16,128,128]{3,2,1,0:T(8,128)S(1)} %fusion.67, ...), kind=kOutput, calls=%fused_computation.1 | convolution fusion | flops 1619542016 | bytes 8717312 | tf_op jit(solution)/shard_map/dot_general | solution.py:59
  54.2 0.0 copy-start.3
  54.2 0.0 copy-start.4
  54.2 0.0 copy-start.5
  54.2 0.3 copy.67
  54.5 1.4 %reshape.232 = f32[8,1,2048]{2,1,0:T(1,128)} reshape(f32[256,2,2,16]{3,2,1,0:T(2,128)S(1)} %bitcast.156) | data formatting | bytes 131072
  55.9 6.0 %all-to-all-start.1 = ((f32[8,1,2048]{2,1,0:T(1,128)}), f32[8,1,2048]{2,1,0:T(1,128)S(1)}, u32[]{:S(2)}, u32[]{:S(2)}) async-start(f32[8,1,2048]{2,1,0:T(1,128)} %reshape.232), calls=%async_computation.1 | async-start | bytes 131072 | tf_op jit(solution)/shard_map/all_to_all | solution.py:82
  61.9 0.1 add_multiply_fusion.1
  62.0 6.8 %all-to-all-done.1 = f32[8,1,2048]{2,1,0:T(1,128)S(1)} async-done(((f32[8,1,2048]{2,1,0:T(1,128)}), f32[8,1,2048]{2,1,0:T(1,128)S(1)}, u32[]{:S(2)}, u32[]{:S(2)}) %all-to-all-start.1) | async-done | bytes 65568 | tf_op jit(solution)/shard_map/all_to_all | solution.py:82
  68.8 0.8 reduce.1
  69.6 0.7 reshape.233
  70.3 0.3 copy.85
  70.6 0.0 copy-start
  70.6 0.0 copy-done.3
  70.7 0.0 copy-done.4
  70.7 0.0 copy-done.5
  70.7 0.6 fusion.88
  71.2 0.6 copy.75
  71.9 5.4 %all_gather.3 = bf16[2,8,32,128]{3,2,0,1:T(8,128)(2,1)S(1)} all-gather(bf16[2,2,32,128]{3,2,0,1:T(8,128)(2,1)S(1)} %get-tuple-element.28), channel_id=1, replica_groups=mesh['pw'=8,'band'=4] {'band'}, dimensions={1}, use_global_device_ids=true | all-gather | bytes 163840 | tf_op jit(solution)/shard_map/all_gather | solution.py:86
  77.3 2.3 %fusion.26 = f32[8,256]{1,0:T(8,128)S(1)} fusion(bf16[1,256,32,128]{3,2,1,0:T(8,128)(2,1)} %get-tuple-element.15, bf16[1,8,32,128]{3,2,0,1:T(8,128)(2,1)S(1)} %get-tuple-element.17), kind=kOutput, calls=%fused_computation.34 | convolution fusion | flops 16777216 | bytes 2170880 | tf_op jit(solution)/shard_map/dot_general | solution.py:92
  79.6 0.0 copy-done
  79.6 0.7 fusion.25
  80.3 0.7 fusion.30
  81.0 0.7 fusion.32
  81.7 33.7 %psum.7 = f32[2,8,256]{2,1,0:T(8,128)S(1)} all-reduce(f32[2,8,256]{2,1,0:T(8,128)S(1)} %pad_maximum_fusion.5), channel_id=1, replica_groups=mesh['pw'=8,'band'=4] {'pw'}, use_global_device_ids=true, to_apply=%region_2.3 | all-reduce | flops 4096 | bytes 32768 | tf_op jit(solution)/shard_map/psum | solution.py:101
  115.3 0.6 constant_dynamic-slice_fusion
  (5 shorter events, 0.0 us)
Async XLA Ops:
  0.6 11.2 %copy-start.6 = (s32[256]{0:T(256)S(1)}, s32[256]{0:T(256)}, u32[]{:S(2)}) copy-start(s32[256]{0:T(256)} %param.7) | copy-start | bytes 3076
  0.6 12.4 %copy-start.2 = (f32[16,128,128]{2,1,0:T(8,128)S(1)}, f32[16,128,128]{2,1,0:T(8,128)}, u32[]{:S(2)}) copy-start(f32[16,128,128]{2,1,0:T(8,128)} %param.6) | copy-start | bytes 3145732
  4.5 15.5 %all-to-all-start = ((f32[8,1,2048]{2,1,0:T(1,128)}), f32[8,1,2048]{2,1,0:T(1,128)}, u32[]{:S(2)}, u32[]{:S(2)}) async-start(f32[8,1,2048]{2,1,0:T(1,128)} %reshape.230), calls=%async_computation | async-start | bytes 131072 | tf_op jit(solution)/shard_map/all_to_all | solution.py:66
  28.1 4.2 %copy-start.1 = (f32[128,256]{1,0:T(8,128)S(1)}, f32[128,256]{1,0:T(8,128)}, u32[]{:S(2)}) copy-start(f32[128,256]{1,0:T(8,128)} %get-tuple-element.27) | copy-start | bytes 393220
  54.2 16.5 %copy-start.3 = (f32[1,2,128,128]{3,2,1,0:T(8,128)S(1)}, f32[1,2,128,128]{3,2,1,0:T(8,128)}, u32[]{:S(2)}) copy-start(f32[1,2,128,128]{3,2,1,0:T(8,128)} %get-tuple-element.18) | copy-start | bytes 393220
  54.2 16.5 %copy-start.4 = (f32[1,2,128,128]{3,2,1,0:T(8,128)S(1)}, f32[1,2,128,128]{3,2,1,0:T(8,128)}, u32[]{:S(2)}) copy-start(f32[1,2,128,128]{3,2,1,0:T(8,128)} %get-tuple-element.19) | copy-start | bytes 393220
  54.2 16.5 %copy-start.5 = (f32[2,2,32,128]{3,2,1,0:T(8,128)S(1)}, f32[2,2,32,128]{3,2,1,0:T(8,128)}, u32[]{:S(2)}) copy-start(f32[2,2,32,128]{3,2,1,0:T(8,128)} %param.4) | copy-start | bytes 196612
  55.9 12.9 %all-to-all-start.1 = ((f32[8,1,2048]{2,1,0:T(1,128)}), f32[8,1,2048]{2,1,0:T(1,128)S(1)}, u32[]{:S(2)}, u32[]{:S(2)}) async-start(f32[8,1,2048]{2,1,0:T(1,128)} %reshape.232), calls=%async_computation.1 | async-start | bytes 131072 | tf_op jit(solution)/shard_map/all_to_all | solution.py:82
  70.6 9.0 %copy-start = (bf16[1,256,32,128]{3,2,1,0:T(8,128)(2,1)S(1)}, bf16[1,256,32,128]{3,2,1,0:T(8,128)(2,1)}, u32[]{:S(2)}) copy-start(bf16[1,256,32,128]{3,2,1,0:T(8,128)(2,1)} %get-tuple-element.15) | copy-start | bytes 6291460
where the time goes:
time: 117 us; the launch traced here: 116 us
  blocking collectives  39.1 us (33%)
  matrix products  31.3 us (27%)
  local copies, waits for them, and re-layouts  17.5 us (15%)
  starting transfers between devices  13.3 us (11%)
  other arithmetic  7.07 us (6%)
  waiting for transfers between devices  6.84 us (6%)
    psum x1, blocking collectives, per_device(): summed = lax.psum(partial_value, 'pw')  33.7 us
    dot_general x12, matrix products, mult(): jnp.dot(left, right, precision=highest, preferred_element_type=jnp.float32)  25.2 us
    all_to_all x1, starting transfers between devices, per_device(): lax.all_to_all(z_lines, 'pw', split_axis=1, concat_axis=3, tiled=True)  7.28 us
    all_to_all x1, waiting for transfers between devices, per_device(): lax.all_to_all(picked, 'pw', split_axis=3, concat_axis=1, tiled=True)  6.83 us
    all_to_all x1, starting transfers between devices, per_device(): lax.all_to_all(picked, 'pw', split_axis=3, concat_axis=1, tiled=True)  5.99 us
    unnamed x19, local copies, waits for them, and re-layouts  5.42 us
    all_gather x1, blocking collectives, per_device(): gathered = lax.all_gather(lowered, 'band', axis=1, tiled=True)  5.41 us
    slice x1, local copies, waits for them, and re-layouts, per_device(): all_re = psi_all[0].reshape(psi_all.shape[1], -1)  4.29 us
  transfers between devices with their start and end apart: 2, of which 1 were waited for; matrix products, arithmetic and copies ran while one was open for 7% of the time, Pallas kernels for 0%

commit v1 on v0

--- a/solution.py
+++ b/solution.py
@@ -3,6 +3,19 @@
 import jax.numpy as jnp
 from jax import lax
 from jax.sharding import PartitionSpec as P
+
+
+def gather_around(x, axis, dim):
+    ways = lax.axis_size(axis)
+    up = [(d, (d + 1) % ways) for d in range(ways)]
+    down = [(d, (d - 1) % ways) for d in range(ways)]
+    earlier, later = ([x], [x])
+    for _ in range(ways // 2):
+        earlier.append(lax.ppermute(earlier[-1], axis, up))
+    for _ in range((ways - 1) // 2):
+        later.append(lax.ppermute(later[-1], axis, down))
+    line = jnp.concatenate([*earlier[::-1], *later[1:]], axis=dim)
+    return jnp.roll(line, (lax.axis_index(axis) - ways // 2) * x.shape[dim], axis=dim)
 
 
 def frequency(index, size):
@@ -83,7 +96,7 @@
     vpsi = jnp.einsum("dcvu,bucs->dbsv", forward, sticks_back, precision=highest)
     applied = kinetic[None, None] * psi_block + vpsi
     lowered = applied.astype(jnp.bfloat16)
-    gathered = lax.all_gather(lowered, "band", axis=1, tiled=True)
+    gathered = gather_around(lowered, "band", 1)
     h_re = gathered[0].reshape(gathered.shape[1], -1)
     h_im = gathered[1].reshape(gathered.shape[1], -1)
     real_part = lax.dot_general(

time: 117 us -> 107 us (0.915)
  waiting for transfers between devices: 6.84 us -> 16.8 us
  local copies, waits for them, and re-layouts: 17.5 us -> 10.7 us
  blocking collectives: 39.1 us -> 33.7 us
  other arithmetic: 7.07 us -> 3.25 us
  matrix products: 31.3 us -> 28.9 us
    all_to_all x1, waiting for transfers between devices: 0.01 us -> 5.79 us  [per_device(): lax.all_to_all(z_lines, 'pw', split_axis=1, concat_axis=3, tiled=True)]
    all_gather x1 -> x0, blocking collectives: 5.41 us -> none  [per_device(): gathered = lax.all_gather(lowered, 'band', axis=1, tiled=True)]
    ppermute x0 -> x3, waiting for transfers between devices: none -> 4.26 us  [the longest x2 3.33 us: gather_around(): earlier.append(lax.ppermute(earlier[-1], axis, up))]
    all_to_all x4, local copies, waits for them, and re-layouts: 3.97 us -> 0.74 us  [per_device(): lax.all_to_all(z_lines, 'pw', split_axis=1, concat_axis=3, tiled=True)]
    all_to_all x1, starting transfers between devices: 5.99 us -> 3.35 us  [per_device(): lax.all_to_all(picked, 'pw', split_axis=3, concat_axis=1, tiled=True)]
    ppermute x0 -> x3, starting transfers between devices: none -> 1.8 us  [the longest x1 1.74 us: gather_around(): later.append(lax.ppermute(later[-1], axis, down))]
    dot_general x1, matrix products: 2.28 us -> 0.7 us  [per_device(): lax.dot_general(h_re, all_im, dims, preferred_element_type=jnp.float32)]
    unnamed x19 -> x20, local copies, waits for them, and re-layouts: 5.42 us -> 3.93 us
  transfers between devices with their start and end apart: 2 -> 5, of which waited for: 1 -> 4; matrix products, arithmetic and copies ran while one was open for 7% -> 6% of each run, Pallas kernels for 0% -> 0%
where the time goes in v1:
time: 107 us
  blocking collectives  33.7 us (31%)
  matrix products  28.9 us (27%)
  waiting for transfers between devices  16.8 us (16%)
  starting transfers between devices  12.4 us (12%)
  local copies, waits for them, and re-layouts  10.7 us (10%)
  other arithmetic  3.25 us (3%)
    psum x1, blocking collectives, per_device(): summed = lax.psum(partial_value, 'pw')  33.7 us
    dot_general x12, matrix products, mult(): jnp.dot(left, right, precision=highest, preferred_element_type=jnp.float32)  24.4 us
    all_to_all x1, starting transfers between devices, per_device(): lax.all_to_all(z_lines, 'pw', split_axis=1, concat_axis=3, tiled=True)  7.28 us
    all_to_all x1, waiting for transfers between devices, per_device(): lax.all_to_all(picked, 'pw', split_axis=3, concat_axis=1, tiled=True)  6.77 us
    all_to_all x1, waiting for transfers between devices, per_device(): lax.all_to_all(z_lines, 'pw', split_axis=1, concat_axis=3, tiled=True)  5.79 us
    slice x1, local copies, waits for them, and re-layouts, per_device(): all_im = psi_all[1].reshape(psi_all.shape[1], -1)  4.3 us
    unnamed x20, local copies, waits for them, and re-layouts  3.93 us
    all_to_all x1, starting transfers between devices, per_device(): lax.all_to_all(picked, 'pw', split_axis=3, concat_axis=1, tiled=True)  3.35 us
  transfers between devices with their start and end apart: 5, of which 4 were waited for; matrix products, arithmetic and copies ran while one was open for 6% of the time, Pallas kernels for 0%

profile of v1, /device:TPU:0, one launch (start us, length us, event | category | flops | bytes accessed | tf_op | source)
XLA Modules:
  0.0 106.8 jit_solution(7088719237774027668)
XLA Ops:
  0.6 0.0 copy-start.3
  0.6 0.0 copy-start.1
  0.6 0.3 fusion.80
  0.9 0.3 fusion.78
  1.2 0.3 broadcast_multiply_fusion
  1.5 1.2 %convolution_bitcast_fusion = f32[2,128,2,32]{1,3,0,2:T(8,128)S(1)} fusion(f32[1,2,128,128]{3,2,1,0:T(8,128)S(1)} %get-tuple-element.20, f32[1,2,128,128]{3,2,1,0:T(8,128)S(1)} %get-tuple-element.21, f32[2,2,32,128]{3,2,1,0:T(8,128)} %param.4), kind=kOutput, calls=%fused_computation.30 | convolution fusion | flops 50397184 | bytes 393216 | tf_op jit(solution)/shard_map/dcvu,cbsu->bvds/dot_general | solution.py:78
  2.7 0.2 copy.67
  2.9 0.9 reshape.230
  3.8 7.3 %all-to-all-start = ((f32[8,1,2048]{2,1,0:T(1,128)}), f32[8,1,2048]{2,1,0:T(1,128)S(1)}, u32[]{:S(2)}, u32[]{:S(2)}) async-start(f32[8,1,2048]{2,1,0:T(1,128)} %reshape.230), calls=%async_computation | async-start | bytes 131072 | tf_op jit(solution)/shard_map/all_to_all | solution.py:79
  11.1 0.0 copy-done.3
  11.1 0.5 fusion.62
  11.7 0.0 copy-done.1
  11.7 0.1 multiply_bitcast_fusion
  11.8 0.3 copy.70
  12.1 0.1 fusion.83
  12.2 5.8 %all-to-all-done = f32[8,1,2048]{2,1,0:T(1,128)S(1)} async-done(((f32[8,1,2048]{2,1,0:T(1,128)}), f32[8,1,2048]{2,1,0:T(1,128)S(1)}, u32[]{:S(2)}, u32[]{:S(2)}) %all-to-all-start) | async-done | bytes 65568 | tf_op jit(solution)/shard_map/all_to_all | solution.py:79
  18.0 0.5 broadcast.385
  18.5 0.8 reduce
  19.3 0.2 reshape.231
  19.6 0.1 copy.69
  19.7 0.1 all_to_all.29
  19.8 2.4 %fusion = f32[2,16,128,128]{3,2,1,0:T(8,128)S(1)} fusion(f32[128,256]{1,0:T(8,128)S(1)} %get-tuple-element.27, f32[2,16,256]{2,1,0:T(8,128)S(1)} %get-tuple-element.23, f32[128,256]{1,0:T(8,128)S(1)} %get-tuple-element.26, f32[2,16,256]{2,1,0:T(8,128)S(1)} %get-tuple-element.22, s32[256]{0:T(256)S(1)} %get-tuple-element.24), kind=kOutput, calls=%fused_computation.2 | convolution fusion | flops 1613791232 | bytes 2425856 | tf_op jit(solution)/shard_map/dot_general | solution.py:72
  22.3 2.4 %fusion.4 = f32[2,16,128,128]{3,2,1,0:T(8,128)S(1)} fusion(f32[128,256]{1,0:T(8,128)S(1)} %get-tuple-element.27, f32[2,16,256]{2,1,0:T(8,128)S(1)} %get-tuple-element.23, f32[128,256]{1,0:T(8,128)S(1)} %get-tuple-element.26, f32[2,16,256]{2,1,0:T(8,128)S(1)} %get-tuple-element.22, s32[256]{0:T(256)S(1)} %get-tuple-element.24), kind=kOutput, calls=%fused_computation.6 | convolution fusion | flops 1613791232 | bytes 2425856 | tf_op jit(solution)/shard_map/dot_general | solution.py:72
  24.7 1.8 %fusion.76 = f32[2,16,128,128]{3,2,1,0:T(8,128)S(1)} fusion(f32[2,16,128,128]{3,2,1,0:T(8,128)S(1)} %fusion.4, f32[1,2,128,128]{3,2,1,0:T(8,128)S(1)} %get-tuple-element.20), kind=kOutput, calls=%fused_computation.100 | convolution fusion | flops 805306368 | bytes 4259840 | tf_op jit(solution)/shard_map/dot_general | solution.py:72
  26.6 1.8 %fusion.73 = f32[2,16,128,128]{3,2,1,0:T(8,128)S(1)} fusion(f32[2,16,128,128]{3,2,1,0:T(8,128)S(1)} %fusion.4, f32[1,2,128,128]{3,2,1,0:T(8,128)S(1)} %get-tuple-element.21), kind=kOutput, calls=%fused_computation.97 | convolution fusion | flops 805306368 | bytes 4259840 | tf_op jit(solution)/shard_map/dot_general | solution.py:72
  28.4 1.9 %subtract_multiply_fusion = f32[2,16,128,128]{3,2,1,0:T(8,128)S(1)} fusion(f32[2,16,128,128]{3,2,1,0:T(8,128)S(1)} %fusion.73, f32[2,16,128,128]{3,2,1,0:T(8,128)S(1)} %fusion, f32[16,128,128]{2,1,0:T(8,128)S(1)} %copy.70, f32[1,2,128,128]{3,2,1,0:T(8,128)S(1)} %get-tuple-element.20), kind=kOutput, calls=%fused_computation.17 | convolution fusion | flops 806354944 | bytes 7405568 | tf_op jit(solution)/shard_map/dot_general | solution.py:72
  30.4 2.0 %fusion.74 = f32[2,16,128,128]{3,2,1,0:T(8,128)S(1)} fusion(f32[2,16,128,128]{3,2,1,0:T(8,128)S(1)} %subtract_multiply_fusion, f32[1,2,128,128]{3,2,1,0:T(8,128)S(1)} %get-tuple-element.20), kind=kOutput, calls=%fused_computation.98 | convolution fusion | flops 805306368 | bytes 4259840 | tf_op jit(solution)/shard_map/dot_general | solution.py:72
  32.4 1.8 %fusion.72 = f32[2,16,128,128]{3,2,1,0:T(8,128)S(1)} fusion(f32[2,16,128,128]{3,2,1,0:T(8,128)S(1)} %subtract_multiply_fusion, f32[1,2,128,128]{3,2,1,0:T(8,128)S(1)} %get-tuple-element.21), kind=kOutput, calls=%fused_computation.96 | convolution fusion | flops 805306368 | bytes 4259840 | tf_op jit(solution)/shard_map/dot_general | solution.py:72
  34.2 1.9 %add_multiply_fusion = f32[2,16,128,128]{3,2,1,0:T(8,128)S(1)} fusion(f32[2,16,128,128]{3,2,1,0:T(8,128)S(1)} %fusion.76, f32[2,16,128,128]{3,2,1,0:T(8,128)S(1)} %fusion, f32[16,128,128]{2,1,0:T(8,128)S(1)} %copy.70, f32[1,2,128,128]{3,2,1,0:T(8,128)S(1)} %get-tuple-element.21), kind=kOutput, calls=%fused_computation.16 | convolution fusion | flops 806354944 | bytes 7405568 | tf_op jit(solution)/shard_map/dot_general | solution.py:72
  36.1 1.8 %fusion.71 = f32[2,16,128,128]{3,2,1,0:T(8,128)S(1)} fusion(f32[2,16,128,128]{3,2,1,0:T(8,128)S(1)} %add_multiply_fusion, f32[1,2,128,128]{3,2,1,0:T(8,128)S(1)} %get-tuple-element.21), kind=kOutput, calls=%fused_computation.95 | convolution fusion | flops 805306368 | bytes 4259840 | tf_op jit(solution)/shard_map/dot_general | solution.py:72
  37.9 1.8 %fusion.75 = f32[2,16,128,128]{3,2,1,0:T(8,128)S(1)} fusion(f32[2,16,128,128]{3,2,1,0:T(8,128)S(1)} %add_multiply_fusion, f32[1,2,128,128]{3,2,1,0:T(8,128)S(1)} %get-tuple-element.20), kind=kOutput, calls=%fused_computation.99 | convolution fusion | flops 805306368 | bytes 4259840 | tf_op jit(solution)/shard_map/dot_general | solution.py:72
  39.8 1.8 %fusion.10 = f32[2,16,128,256]{3,2,1,0:T(8,128)S(1)} fusion(f32[2,16,128,128]{3,2,1,0:T(8,128)S(1)} %fusion.72, f32[2,16,128,128]{3,2,1,0:T(8,128)S(1)} %fusion.75, s32[256]{0:T(256)S(1)} %get-tuple-element.24), kind=kOutput, calls=%fused_computation.14 | convolution fusion | flops 1611169792 | bytes 8389632 | tf_op jit(solution)/shard_map/dot_general | solution.py:72
  41.6 2.8 %add_reduce_fusion = (f32[2,16,256]{2,1,0:T(8,128)S(1)}, f32[2,16,256]{2,1,0:T(8,128)S(1)}) fusion(f32[2,16,128,256]{3,2,1,0:T(8,128)S(1)} %fusion.10, f32[128,256]{1,0:T(8,128)S(1)} %get-tuple-element.27, f32[128,256]{1,0:T(8,128)S(1)} %get-tuple-element.26, s32[256]{0:T(256)S(1)} %get-tuple-element.24, f32[2,16,128,128]{3,2,1,0:T(8,128)S(1)} %fusion.71, ...), kind=kOutput, calls=%fused_computation.1 | convolution fusion | flops 1619542016 | bytes 8717312 | tf_op jit(solution)/shard_map/dot_general | solution.py:72
  44.4 0.0 copy-start.2
  44.4 0.3 copy.71
  44.7 1.4 %reshape.232 = f32[8,1,2048]{2,1,0:T(1,128)} reshape(f32[256,2,2,16]{3,2,1,0:T(2,128)S(1)} %bitcast.152) | data formatting | bytes 131072
  46.1 3.4 %all-to-all-start.1 = ((f32[8,1,2048]{2,1,0:T(1,128)}), f32[8,1,2048]{2,1,0:T(1,128)S(1)}, u32[]{:S(2)}, u32[]{:S(2)}) async-start(f32[8,1,2048]{2,1,0:T(1,128)} %reshape.232), calls=%async_computation.1 | async-start | bytes 131072 | tf_op jit(solution)/shard_map/all_to_all | solution.py:95
  49.4 0.1 add_multiply_fusion.1
  49.5 6.8 %all-to-all-done.1 = f32[8,1,2048]{2,1,0:T(1,128)S(1)} async-done(((f32[8,1,2048]{2,1,0:T(1,128)}), f32[8,1,2048]{2,1,0:T(1,128)S(1)}, u32[]{:S(2)}, u32[]{:S(2)}) %all-to-all-start.1) | async-done | bytes 65568 | tf_op jit(solution)/shard_map/all_to_all | solution.py:95
  56.3 0.8 reduce.1
  57.1 0.7 reshape.233
  57.8 0.3 copy.91
  58.1 0.0 copy-done.2
  58.1 0.6 fusion.91
  58.7 0.1 collective-permute-start
  58.8 3.3 %collective-permute-done = bf16[2,2,32,128]{3,2,0,1:T(8,128)(2,1)S(1)} collective-permute-done((bf16[2,2,32,128]{3,2,0,1:T(8,128)(2,1)S(1)}, bf16[2,2,32,128]{3,2,0,1:T(8,128)(2,1)S(1)}, u32[]{:S(2)}, u32[]{:S(2)}) %collective-permute-start) | collective-permute-done | bytes 32800 | tf_op jit(solution)/shard_map/ppermute | solution.py:14
  62.1 0.0 collective-permute-start.1
  62.1 4.3 %fusion.90 = (bf16[1,256,32,128]{3,2,1,0:T(8,128)(2,1)S(1)}, bf16[1,256,32,128]{3,2,1,0:T(8,128)(2,1)}) fusion(bf16[2,256,32,128]{3,2,1,0:T(8,128)(2,1)} %param.5), kind=kLoop, calls=%fused_computation.143 | loop fusion | bytes 8388608 | tf_op jit(solution)/shard_map/slice | solution.py:75
  66.4 0.0 copy-start
  66.4 1.7 %collective-permute-start.2 = (bf16[2,2,32,128]{3,2,0,1:T(8,128)(2,1)S(1)}, bf16[2,2,32,128]{3,2,0,1:T(8,128)(2,1)S(1)}, u32[]{:S(2)}, u32[]{:S(2)}) collective-permute-start(bf16[2,2,32,128]{3,2,0,1:T(8,128)(2,1)S(1)} %get-tuple-element.28), channel_id=1, source_target_pairs={{0,3},{1,0},{2,1},{3,2},{4,7},{5,4},{6,5},{7,6},{8,11},{9,8},{10,9... | collective-permute-start | bytes 98312 | tf_op jit(solution)/shard_map/ppermute | solution.py:16
  68.1 0.6 copy.81
  68.8 0.0 collective-permute-done.1
  68.8 0.9 collective-permute-done.2
  69.8 0.7 fusion.25
  70.5 0.0 copy-done
  70.5 0.7 fusion.28
  71.2 0.7 fusion.30
  71.9 0.7 fusion.32
  72.6 33.7 %psum.7 = f32[2,8,256]{2,1,0:T(8,128)S(1)} all-reduce(f32[2,8,256]{2,1,0:T(8,128)S(1)} %pad_maximum_fusion.5), channel_id=1, replica_groups=mesh['pw'=8,'band'=4] {'pw'}, use_global_device_ids=true, to_apply=%region_2.3 | all-reduce | flops 4096 | bytes 32768 | tf_op jit(solution)/shard_map/psum | solution.py:114
  106.2 0.6 constant_dynamic-slice_fusion
  (16 shorter events, 0.2 us)
Async XLA Ops:
  0.6 10.5 %copy-start.3 = (s32[256]{0:T(256)S(1)}, s32[256]{0:T(256)}, u32[]{:S(2)}) copy-start(s32[256]{0:T(256)} %param.7) | copy-start | bytes 3076
  0.6 11.0 %copy-start.1 = (f32[16,128,128]{2,1,0:T(8,128)S(1)}, f32[16,128,128]{2,1,0:T(8,128)}, u32[]{:S(2)}) copy-start(f32[16,128,128]{2,1,0:T(8,128)} %param.6) | copy-start | bytes 3145732
  3.8 14.2 %all-to-all-start = ((f32[8,1,2048]{2,1,0:T(1,128)}), f32[8,1,2048]{2,1,0:T(1,128)S(1)}, u32[]{:S(2)}, u32[]{:S(2)}) async-start(f32[8,1,2048]{2,1,0:T(1,128)} %reshape.230), calls=%async_computation | async-start | bytes 131072 | tf_op jit(solution)/shard_map/all_to_all | solution.py:79
  44.4 13.7 %copy-start.2 = (f32[2,2,32,128]{3,2,1,0:T(8,128)S(1)}, f32[2,2,32,128]{3,2,1,0:T(8,128)}, u32[]{:S(2)}) copy-start(f32[2,2,32,128]{3,2,1,0:T(8,128)} %param.4) | copy-start | bytes 196612
  46.1 10.2 %all-to-all-start.1 = ((f32[8,1,2048]{2,1,0:T(1,128)}), f32[8,1,2048]{2,1,0:T(1,128)S(1)}, u32[]{:S(2)}, u32[]{:S(2)}) async-start(f32[8,1,2048]{2,1,0:T(1,128)} %reshape.232), calls=%async_computation.1 | async-start | bytes 131072 | tf_op jit(solution)/shard_map/all_to_all | solution.py:95
  58.7 3.4 %collective-permute-start = (bf16[2,2,32,128]{3,2,0,1:T(8,128)(2,1)S(1)}, bf16[2,2,32,128]{3,2,0,1:T(8,128)(2,1)S(1)}, u32[]{:S(2)}, u32[]{:S(2)}) collective-permute-start(bf16[2,2,32,128]{3,2,0,1:T(8,128)(2,1)S(1)} %get-tuple-element.28), channel_id=1, source_target_pairs={{0,1},{1,2},{2,3},{3,0},{4,5},{5,6},{6,7},{7,4},{8,9},{9,10},{10,1... | collective-permute-start | bytes 98312 | tf_op jit(solution)/shard_map/ppermute | solution.py:14
  62.1 6.7 %collective-permute-start.1 = (bf16[2,2,32,128]{3,2,0,1:T(8,128)(2,1)S(1)}, bf16[2,2,32,128]{3,2,0,1:T(8,128)(2,1)S(1)}, u32[]{:S(2)}, u32[]{:S(2)}) collective-permute-start(bf16[2,2,32,128]{3,2,0,1:T(8,128)(2,1)S(1)} %collective-permute-done), channel_id=1, source_target_pairs={{0,1},{1,2},{2,3},{3,0},{4,5},{5,6},{6,7},{7,4},{8,9},{9,10},{10,1... | collective-permute-start | bytes 98312 | tf_op jit(solution)/shard_map/ppermute | solution.py:14
  66.4 4.1 %copy-start = (bf16[1,256,32,128]{3,2,1,0:T(8,128)(2,1)S(1)}, bf16[1,256,32,128]{3,2,1,0:T(8,128)(2,1)}, u32[]{:S(2)}) copy-start(bf16[1,256,32,128]{3,2,1,0:T(8,128)(2,1)} %get-tuple-element.15) | copy-start | bytes 6291460
  66.4 3.3 %collective-permute-start.2 = (bf16[2,2,32,128]{3,2,0,1:T(8,128)(2,1)S(1)}, bf16[2,2,32,128]{3,2,0,1:T(8,128)(2,1)S(1)}, u32[]{:S(2)}, u32[]{:S(2)}) collective-permute-start(bf16[2,2,32,128]{3,2,0,1:T(8,128)(2,1)S(1)} %get-tuple-element.28), channel_id=1, source_target_pairs={{0,3},{1,0},{2,1},{3,2},{4,7},{5,4},{6,5},{7,6},{8,11},{9,8},{10,9... | collective-permute-start | bytes 98312 | tf_op jit(solution)/shard_map/ppermute | solution.py:16
